TPU v7x, 32 devices: a whole 2x2x4 slice. The times are simulated.
32 devices in a mesh: island: 4 (over z), fsdp: 8 (over y, x, core).
Axes of the slice: x: 2, y: 2, z: 4, core: 2. Of those that a mesh axis runs over, the one named last changes fastest.
Arguments:
- activations: bfloat16 [4, 4096, 8192], P('island', 'fsdp'), may hold values from -150 to 150
- key_cotangents: bfloat16 [4, 4096, 512], P('island', 'fsdp'), may hold values from -60 to 60
- master: float32 [8192, 512], P('fsdp'), may hold values from -6 to 6
- momentum: float32 [8192, 512], P('fsdp'), may hold values from -3 to 3
- island_weights: float32 [4, 8192, 512], P('island', 'fsdp'), may hold values from -6 to 6
- first_moment: float32 [4, 8192, 512], P('island', 'fsdp'), may hold values from -0.0024414062 to 0.0024414062
- second_moment: float32 [4, 8192, 512], P('island', 'fsdp'), may hold values from 5.9604645e-08 to 9.536743e-07
- tile_rows: int32 [48], replicated, may hold values from 1 to 512, 8192 in all
Outputs:
- master_out: float32 [8192, 512], P('fsdp')
- momentum_out: float32 [8192, 512], P('fsdp')
- tile_sums: float32 [48], replicated
Inputs may be any that keep to these rules, and one draw needn't show every extreme that they name: `tile_rows`: consecutive tiles covering all 8192 rows; the largest has exactly 512 rows.
All inputs are finite; a program needn't handle non-finite values.
Results may differ from a plain program's by a relative error of at most 0.0003.
Values may be sent and summed in bfloat16 or wider, within the bound.
No kernel may reach another device: no remote copies, remote signals or barrier semaphores. Data moves between devices by JAX's collectives and lax.ppermute only.
A program may use at most 128 MiB of HBM per device.

v0:
```python
import jax
import jax.numpy as jnp
from jax import lax
from jax.experimental.layout import Layout, with_layout_constraint
from jax.sharding import PartitionSpec as P

HEAD = 128
SEQ = 8192
beta_one = 0.9
beta_two = 0.95
bias_one = 1.0 - 0.9**3
bias_two = 1.0 - 0.95**3
inner_rate = 0.5
decay_rate = 0.1
outer_rate = 0.7
outer_moment = 0.9
adam_eps = 1e-08
norm_epsilon = 1e-06
rope_base = 500000.0


def unrotate(cotangent, first_row):
    rows = cotangent.shape[0]
    half = HEAD // 2
    positions = ((first_row + jnp.arange(rows, dtype=jnp.int32)) % SEQ).astype(jnp.float32)
    rates = rope_base ** (-2.0 * jnp.arange(half).astype(jnp.float32) / HEAD)
    angles = positions[:, None] * rates[None, :]
    cosine = jnp.cos(angles)[:, None, :]
    sine = jnp.sin(angles)[:, None, :]
    heads = cotangent.astype(jnp.float32).reshape(rows, -1, HEAD)
    lower = heads[:, :, :half]
    upper = heads[:, :, half:]
    turned = jnp.concatenate([lower * cosine + upper * sine, upper * cosine - lower * sine], axis=2)
    return turned.reshape(rows, -1).astype(jnp.bfloat16)


def adam_update(gradient, weights, first, second):
    first_new = beta_one * first + (1.0 - beta_one) * gradient
    second_new = beta_two * second + (1.0 - beta_two) * gradient * gradient
    ratio = first_new / bias_one / (jnp.sqrt(second_new / bias_two) + adam_eps)
    return weights - inner_rate * (ratio + decay_rate * weights)


def local_tiles(drift_rows, tile_rows, first_row):
    ends = jnp.cumsum(tile_rows, dtype=jnp.int32)
    starts = ends - tile_rows
    rows = first_row + jnp.arange(drift_rows.shape[0], dtype=jnp.int32)
    member = ((rows[:, None] >= starts[None, :]) & (rows[:, None] < ends[None, :])).astype(
        jnp.float32
    )
    return jnp.dot(jnp.sum(drift_rows, axis=1), member, precision=lax.Precision.HIGHEST)


def island_sum(values, replicas, pieces=4):
    if replicas != 4:
        return lax.psum(values, "island")
    island = lax.axis_index("island")
    middle = (island == 1) | (island == 2)
    rows = values.shape[0] // pieces
    sums, arrived = ([], None)
    for piece in range(pieces):
        part = values[piece * rows : (piece + 1) * rows]
        if arrived is not None:
            part, _ = lax.optimization_barrier((part, arrived))
        arrived = lax.ppermute(part, "island", [(0, 1), (3, 2)])
        pair = part + arrived
        whole = pair + lax.ppermute(pair, "island", [(1, 2), (2, 1)])
        back = lax.ppermute(whole, "island", [(1, 0), (2, 3)])
        sums.append(jnp.where(middle, whole, back))
    return jnp.concatenate(sums, axis=0)


def body(
    activations,
    key_cotangents,
    master,
    momentum,
    island_weights,
    first_moment,
    second_moment,
    tile_rows,
):
    own_rows = master.shape[0]
    tok_rows = key_cotangents.shape[1]
    chips = lax.axis_size("chip")
    core = lax.axis_index("core")
    position = lax.axis_index("chip") * 2 + core
    swap = [(0, 1), (1, 0)]
    unrotated = unrotate(key_cotangents[0], position * tok_rows)
    tokens = activations[0]

    def parity(side):
        return jnp.stack(
            [
                lax.dynamic_slice_in_dim(tokens, (2 * k + side) * own_rows, own_rows, axis=1)
                for k in range(chips)
            ],
            axis=1,
        )

    their_tokens = lax.ppermute(parity(1 - core), "core", swap)
    their_unrotated = lax.ppermute(unrotated, "core", swap)
    contract = (((0,), (0,)), ((), ()))
    partial = lax.dot_general(
        unrotated, parity(core), contract, preferred_element_type=jnp.float32
    ) + lax.dot_general(their_unrotated, their_tokens, contract, preferred_element_type=jnp.float32)
    gradient = lax.psum_scatter(partial, "chip", scatter_dimension=1, tiled=True)
    gradient = with_layout_constraint(gradient, Layout((0, 1, 2)))
    gradient = with_layout_constraint(
        gradient.reshape(gradient.shape[0], own_rows).T, Layout((0, 1))
    )
    squares = lax.psum(jnp.sum(gradient * gradient), ("chip", "core"))
    factor = 1.0 / jnp.sqrt(squares + norm_epsilon)
    inner = adam_update(gradient * factor, island_weights[0], first_moment[0], second_moment[0])
    island_drift = master - inner
    replicas = lax.axis_size("island")
    first_row = position * own_rows
    everyone = ("island", "chip", "core")
    partials = local_tiles(island_drift, tile_rows, first_row)
    padded = jnp.zeros((65536,), jnp.float32).at[: partials.shape[0]].set(partials)
    totals = lax.psum(padded, everyone)[: partials.shape[0]] / replicas
    drift = island_sum(island_drift, replicas) / replicas
    momentum_out = outer_moment * momentum + drift
    master_out = master - outer_rate * (drift + outer_moment * momentum_out)
    tile_sums = totals / jnp.sqrt(tile_rows.astype(jnp.float32) * master.shape[1])
    return (master_out, momentum_out, tile_sums)


def solution(mesh):
    islands, fsdp = mesh.devices.shape
    cores = jax.sharding.Mesh(
        mesh.devices.reshape(islands, fsdp // 2, 2), ("island", "chip", "core")
    )
    rows = ("chip", "core")
    placed = (
        P("island", rows, None),
        P("island", rows, None),
        P(rows, None),
        P(rows, None),
        P("island", rows, None),
        P("island", rows, None),
        P("island", rows, None),
        P(),
    )
    return jax.shard_map(
        body,
        mesh=cores,
        in_specs=placed,
        out_specs=(P(rows, None), P(rows, None), P()),
        check_vma=False,
    )
```

profile of v0, /device:TPU:0, one launch (start us, length us, event | category | flops | bytes accessed | tf_op | source)
XLA Modules:
  0.0 363.9 jit_solution(9505688208822841466)
XLA Ops:
  7.2 5.7 %dynamic-slice_bitcast_fusion.3 = (bf16[512,1,1024]{2,0,1:T(8,128)(2,1)S(1)}, bf16[512,1,1024]{2,0,1:T(8,128)(2,1)S(1)}, bf16[512,1,1024]{2,0,1:T(8,128)(2,1)S(1...) fusion(bf16[1,512,8192]{2,1,0:T(8,128)(2,1)} %param.10, ...), kind=kLoop, calls=%fused_computation.32 | loop fusion | bytes 16777248 | tf_op jit(solution)/shard_map/stack | solution.py:93
  13.0 2.2 pad_maximum_fusion
  15.2 0.5 collective-permute-start.1
  15.6 1.3 copy.29
  16.9 0.5 multiply_cosine_fusion
  17.5 0.2 add_convert_fusion
  17.7 0.1 collective-permute-start
  17.8 0.3 copy-done.2
  18.1 0.3 copy-done.3
  18.4 2.5 fusion
  20.9 2.2 collective-permute-done
  23.1 7.9 %convolution_add_fusion = f32[512,4,1024]{2,0,1:T(8,128)} fusion(f32[512,4,1024]{2,0,1:T(8,128)S(1)} %fusion, bf16[512,4,1024]{2,0,1:T(8,128)(2,1)} %collective-permute-done.1, bf16[512,512]{0,1:T(8,128)(2,1)S(1)} %collective-permute-done), kind=kOutput, calls=%fused_computation.10 | convolution fusion | flops 2149580800 | bytes 21495808 | tf_op jit(solution)/shard_map/dot_general | solution.py:106
  31.1 89.1 %reduce-scatter.4.cloned.1.call-done = f32[512,1,1024]{2,0,1:T(8,128)} async-done(((f32[512,4,1024]{2,0,1:T(8,128)}), f32[512,1,1024]{2,0,1:T(8,128)}) %reduce-scatter.4.cloned.1.call-update) | async-done | bytes 2097168
  120.2 1.9 copy.26
  122.1 1.1 fusion.14
  123.3 13.3 %psum.14 = f32[]{:T(128)} all-reduce(f32[]{:T(128)} %fusion.14), channel_id=1, replica_groups=mesh['island'=4,'chip'=4,'core'=2] {'chip','core'}, use_global_device_ids=true, to_apply=%region_2.3 | all-reduce | flops 1 | bytes 8 | tf_op jit(solution)/shard_map/psum | solution.py:112
  137.2 5.4 %fusion.26 = (f32[1024]{0:T(1024)S(1)}, f32[1024,512]{1,0:T(8,128)S(1)}) fusion(f32[1024,512]{1,0:T(8,128)} %param.12, f32[1,1024,512]{2,1,0:T(8,128)} %param.16, f32[]{:T(128)S(6)} %sqrt.9, f32[512,1,1024]{0,2,1:T(8,128)S(1)} %copy.26, f32[1,1024,512]{2,1,0:T(8,128)} %param.15, f32[1,1024,512]{2,1,0:T(8,128)} %param.14), kind=kLoop, calls=%fused_computation.63 | loop fusion | flops 9436160 | bytes 12587012 | tf_op jit(solution)/shard_map/reduce_sum | solution.py:51
  142.7 3.4 collective-permute-start.2
  146.1 10.3 %collective-permute-done.2 = f32[256,512]{1,0:T(8,128)S(1)} collective-permute-done((f32[256,512]{1,0:T(8,128)S(1)}, f32[256,512]{1,0:T(8,128)S(1)}, u32[]{:S(2)}, u32[]{:S(2)}) %collective-permute-start.2) | collective-permute-done | bytes 524320 | tf_op jit(solution)/shard_map/ppermute | solution.py:65
  156.4 0.3 slice_add_fusion
  156.7 4.4 %collective-permute-start.5 = (f32[256,512]{1,0:T(8,128)S(1)}, f32[256,512]{1,0:T(8,128)S(1)}, u32[]{:S(2)}, u32[]{:S(2)}) collective-permute-start(f32[256,512]{1,0:T(8,128)S(1)} %get-tuple-element.18), channel_id=1, source_target_pairs={{0,8},{24,16},{1,9},{25,17},{2,10},{26,18},{3,11},{27,19},{4,12},{... | collective-permute-start | bytes 1572872 | tf_op jit(solution)/shard_map/ppermute | solution.py:65
  161.1 9.4 %collective-permute-done.5 = f32[256,512]{1,0:T(8,128)S(1)} collective-permute-done((f32[256,512]{1,0:T(8,128)S(1)}, f32[256,512]{1,0:T(8,128)S(1)}, u32[]{:S(2)}, u32[]{:S(2)}) %collective-permute-start.5) | collective-permute-done | bytes 524320 | tf_op jit(solution)/shard_map/ppermute | solution.py:65
  170.5 4.4 %collective-permute-start.8 = (f32[256,512]{1,0:T(8,128)S(1)}, f32[256,512]{1,0:T(8,128)S(1)}, u32[]{:S(2)}, u32[]{:S(2)}) collective-permute-start(f32[256,512]{1,0:T(8,128)S(1)} %get-tuple-element.19), channel_id=1, source_target_pairs={{0,8},{24,16},{1,9},{25,17},{2,10},{26,18},{3,11},{27,19},{4,12},{... | collective-permute-start | bytes 1572872 | tf_op jit(solution)/shard_map/ppermute | solution.py:65
  174.9 1.5 collective-permute-start.3
  176.4 7.0 %collective-permute-done.8 = f32[256,512]{1,0:T(8,128)S(1)} collective-permute-done((f32[256,512]{1,0:T(8,128)S(1)}, f32[256,512]{1,0:T(8,128)S(1)}, u32[]{:S(2)}, u32[]{:S(2)}) %collective-permute-start.8) | collective-permute-done | bytes 524320 | tf_op jit(solution)/shard_map/ppermute | solution.py:65
  183.4 5.4 %collective-permute-start.11 = (f32[256,512]{1,0:T(8,128)S(1)}, f32[256,512]{1,0:T(8,128)}, u32[]{:S(2)}, u32[]{:S(2)}) collective-permute-start(f32[256,512]{1,0:T(8,128)S(1)} %get-tuple-element.20), channel_id=1, source_target_pairs={{0,8},{24,16},{1,9},{25,17},{2,10},{26,18},{3,11},{27,19},{4,12},{... | collective-permute-start | bytes 1572872 | tf_op jit(solution)/shard_map/ppermute | solution.py:65
  188.8 1.4 collective-permute-start.6
  190.2 1.1 add.169
  191.4 1.3 collective-permute-start.4
  192.8 0.7 collective-permute-start.9
  193.7 0.1 reduce.2
  193.8 0.4 convolution_bitcast_fusion
  194.2 0.7 scatter.4
  194.9 0.6 collective-permute-done.11
  195.5 1.1 add.174
  196.7 1.5 collective-permute-start.12
  198.2 1.1 add.171
  199.3 1.3 collective-permute-start.7
  200.6 126.3 %all-reduce.4.cloned.1.call-done = f32[65536]{0:T(1024)} async-done(((f32[65536]{0:T(1024)}), f32[65536]{0:T(1024)}) %all-reduce.4.cloned.1.call-update) | async-done | bytes 262160 | tf_op jit(solution)/shard_map/psum | solution.py:121
  326.9 1.2 fusion.24
  328.2 1.3 collective-permute-start.10
  329.5 1.1 broadcast_select_fusion.3
  330.6 1.1 add.175
  331.8 1.6 collective-permute-start.13
  333.3 1.1 broadcast_select_fusion.2
  334.5 10.4 %collective-permute-done.10 = f32[256,512]{1,0:T(8,128)S(1)} collective-permute-done((f32[256,512]{1,0:T(8,128)S(1)}, f32[256,512]{1,0:T(8,128)S(1)}, u32[]{:S(2)}, u32[]{:S(2)}) %collective-permute-start.10) | collective-permute-done | bytes 524320 | tf_op jit(solution)/shard_map/ppermute | solution.py:68
  345.0 9.2 %collective-permute-done.13 = f32[256,512]{1,0:T(8,128)S(1)} collective-permute-done((f32[256,512]{1,0:T(8,128)S(1)}, f32[256,512]{1,0:T(8,128)S(1)}, u32[]{:S(2)}, u32[]{:S(2)}) %collective-permute-start.13) | collective-permute-done | bytes 524320 | tf_op jit(solution)/shard_map/ppermute | solution.py:68
  354.3 2.8 multiply_subtract_fusion
  (32 shorter events, 0.8 us)
Async XLA Ops:
  7.2 113.1 %reduce-scatter.4.cloned.1.call-start = ((), (), s32[]{:S(2)}) async-start(), calls=%async_computation.2 | async-start | bytes 10485760
  15.2 8.0 %collective-permute-start.1 = (bf16[512,4,1024]{2,0,1:T(8,128)(2,1)}, bf16[512,4,1024]{2,0,1:T(8,128)(2,1)}, u32[]{:S(2)}, u32[]{:S(2)}) collective-permute-start(bf16[512,4,1024]{2,0,1:T(8,128)(2,1)} %pad_maximum_fusion), channel_id=1, source_target_pairs={{0,1},{1,0},{2,3},{3,2},{4,5},{5,4},{6,7},{7,6},{8,9},{9,8},{10,11... | collective-permute-start | bytes 12582920 | tf_op jit(solution)/shard_map/ppermute | solution.py:101
  16.9 1.2 copy-start.2
  16.9 1.5 copy-start.3
  17.7 5.5 %collective-permute-start = (bf16[512,512]{0,1:T(8,128)(2,1)S(1)}, bf16[512,512]{0,1:T(8,128)(2,1)S(1)}, u32[]{:S(2)}, u32[]{:S(2)}) collective-permute-start(bf16[512,512]{0,1:T(8,128)(2,1)S(1)} %bitcast.66), channel_id=1, source_target_pairs={{0,1},{1,0},{2,3},{3,2},{4,5},{5,4},{6,7},{7,6},{8,9},{9,8},{10,11... | collective-permute-start | bytes 1572872 | tf_op jit(solution)/shard_map/ppermute | solution.py:102
  31.0 295.9 %all-reduce.4.cloned.1.call-start = ((), (), s32[]{:S(2)}) async-start(), calls=%async_computation.1 | async-start | bytes 524288 | tf_op jit(solution)/shard_map/psum | solution.py:121
  142.7 13.7 %collective-permute-start.2 = (f32[256,512]{1,0:T(8,128)S(1)}, f32[256,512]{1,0:T(8,128)S(1)}, u32[]{:S(2)}, u32[]{:S(2)}) collective-permute-start(f32[256,512]{1,0:T(8,128)S(1)} %slice.41), channel_id=1, source_target_pairs={{0,8},{24,16},{1,9},{25,17},{2,10},{26,18},{3,11},{27,19},{4,12},{... | collective-permute-start | bytes 1572872 | tf_op jit(solution)/shard_map/ppermute | solution.py:65
  156.7 13.8 %collective-permute-start.5 = (f32[256,512]{1,0:T(8,128)S(1)}, f32[256,512]{1,0:T(8,128)S(1)}, u32[]{:S(2)}, u32[]{:S(2)}) collective-permute-start(f32[256,512]{1,0:T(8,128)S(1)} %get-tuple-element.18), channel_id=1, source_target_pairs={{0,8},{24,16},{1,9},{25,17},{2,10},{26,18},{3,11},{27,19},{4,12},{... | collective-permute-start | bytes 1572872 | tf_op jit(solution)/shard_map/ppermute | solution.py:65
  170.5 12.9 %collective-permute-start.8 = (f32[256,512]{1,0:T(8,128)S(1)}, f32[256,512]{1,0:T(8,128)S(1)}, u32[]{:S(2)}, u32[]{:S(2)}) collective-permute-start(f32[256,512]{1,0:T(8,128)S(1)} %get-tuple-element.19), channel_id=1, source_target_pairs={{0,8},{24,16},{1,9},{25,17},{2,10},{26,18},{3,11},{27,19},{4,12},{... | collective-permute-start | bytes 1572872 | tf_op jit(solution)/shard_map/ppermute | solution.py:65
  174.9 15.3 %collective-permute-start.3 = (f32[256,512]{1,0:T(8,128)S(1)}, f32[256,512]{1,0:T(8,128)}, u32[]{:S(2)}, u32[]{:S(2)}) collective-permute-start(f32[256,512]{1,0:T(8,128)S(1)} %get-tuple-element.33), channel_id=1, source_target_pairs={{8,16},{16,8},{9,17},{17,9},{10,18},{18,10},{11,19},{19,11},{12,20... | collective-permute-start | bytes 1572872 | tf_op jit(solution)/shard_map/ppermute | solution.py:67
  183.4 10.1 %copy-start.4 = (s32[48]{0:T(128)S(1)}, s32[48]{0:T(128)}, u32[]{:S(2)}) copy-start(s32[48]{0:T(128)} %param.17) | copy-start | bytes 580
  183.4 12.2 %collective-permute-start.11 = (f32[256,512]{1,0:T(8,128)S(1)}, f32[256,512]{1,0:T(8,128)}, u32[]{:S(2)}, u32[]{:S(2)}) collective-permute-start(f32[256,512]{1,0:T(8,128)S(1)} %get-tuple-element.20), channel_id=1, source_target_pairs={{0,8},{24,16},{1,9},{25,17},{2,10},{26,18},{3,11},{27,19},{4,12},{... | collective-permute-start | bytes 1572872 | tf_op jit(solution)/shard_map/ppermute | solution.py:65
  188.8 9.4 %collective-permute-start.6 = (f32[256,512]{1,0:T(8,128)S(1)}, f32[256,512]{1,0:T(8,128)}, u32[]{:S(2)}, u32[]{:S(2)}) collective-permute-start(f32[256,512]{1,0:T(8,128)S(1)} %add.170), channel_id=1, source_target_pairs={{8,16},{16,8},{9,17},{17,9},{10,18},{18,10},{11,19},{19,11},{12,20... | collective-permute-start | bytes 1572872 | tf_op jit(solution)/shard_map/ppermute | solution.py:67
  191.4 138.1 %collective-permute-start.4 = (f32[256,512]{1,0:T(8,128)S(1)}, f32[256,512]{1,0:T(8,128)}, u32[]{:S(2)}, u32[]{:S(2)}) collective-permute-start(f32[256,512]{1,0:T(8,128)S(1)} %add.169), channel_id=1, source_target_pairs={{8,0},{16,24},{9,1},{17,25},{10,2},{18,26},{11,3},{19,27},{12,4},{... | collective-permute-start | bytes 1572872 | tf_op jit(solution)/shard_map/ppermute | solution.py:68
  192.8 135.3 %collective-permute-start.9 = (f32[256,512]{1,0:T(8,128)S(1)}, f32[256,512]{1,0:T(8,128)S(1)}, u32[]{:S(2)}, u32[]{:S(2)}) collective-permute-start(f32[256,512]{1,0:T(8,128)S(1)} %add.172), channel_id=1, source_target_pairs={{8,16},{16,8},{9,17},{17,9},{10,18},{18,10},{11,19},{19,11},{12,20... | collective-permute-start | bytes 1572872 | tf_op jit(solution)/shard_map/ppermute | solution.py:67
  196.7 134.0 %collective-permute-start.12 = (f32[256,512]{1,0:T(8,128)S(1)}, f32[256,512]{1,0:T(8,128)}, u32[]{:S(2)}, u32[]{:S(2)}) collective-permute-start(f32[256,512]{1,0:T(8,128)S(1)} %add.174), channel_id=1, source_target_pairs={{8,16},{16,8},{9,17},{17,9},{10,18},{18,10},{11,19},{19,11},{12,20... | collective-permute-start | bytes 1572872 | tf_op jit(solution)/shard_map/ppermute | solution.py:67
  199.3 134.1 %collective-permute-start.7 = (f32[256,512]{1,0:T(8,128)S(1)}, f32[256,512]{1,0:T(8,128)}, u32[]{:S(2)}, u32[]{:S(2)}) collective-permute-start(f32[256,512]{1,0:T(8,128)S(1)} %add.171), channel_id=1, source_target_pairs={{8,0},{16,24},{9,1},{17,25},{10,2},{18,26},{11,3},{19,27},{12,4},{... | collective-permute-start | bytes 1572872 | tf_op jit(solution)/shard_map/ppermute | solution.py:68
  328.2 16.8 %collective-permute-start.10 = (f32[256,512]{1,0:T(8,128)S(1)}, f32[256,512]{1,0:T(8,128)S(1)}, u32[]{:S(2)}, u32[]{:S(2)}) collective-permute-start(f32[256,512]{1,0:T(8,128)S(1)} %add.173), channel_id=1, source_target_pairs={{8,0},{16,24},{9,1},{17,25},{10,2},{18,26},{11,3},{19,27},{12,4},{... | collective-permute-start | bytes 1572872 | tf_op jit(solution)/shard_map/ppermute | solution.py:68
  331.7 22.5 %copy-start = (f32[1024,512]{1,0:T(8,128)S(1)}, f32[1024,512]{1,0:T(8,128)}, u32[]{:S(2)}) copy-start(f32[1024,512]{1,0:T(8,128)} %param.12) | copy-start | bytes 6291460
  331.8 22.5 %copy-start.1 = (f32[1024,512]{1,0:T(8,128)S(1)}, f32[1024,512]{1,0:T(8,128)}, u32[]{:S(2)}) copy-start(f32[1024,512]{1,0:T(8,128)} %param.13) | copy-start | bytes 6291460
  331.8 22.4 %collective-permute-start.13 = (f32[256,512]{1,0:T(8,128)S(1)}, f32[256,512]{1,0:T(8,128)S(1)}, u32[]{:S(2)}, u32[]{:S(2)}) collective-permute-start(f32[256,512]{1,0:T(8,128)S(1)} %add.175), channel_id=1, source_target_pairs={{8,0},{16,24},{9,1},{17,25},{10,2},{18,26},{11,3},{19,27},{12,4},{... | collective-permute-start | bytes 1572872 | tf_op jit(solution)/shard_map/ppermute | solution.py:68
Sparse Core Ops, SparseCore 0:
  31.2 89.0 reduce-scatter.3
  195.0 131.8 all-reduce.3
where the time goes:
time: 365 us; the launch traced here: 364 us
  waiting for transfers between devices  265 us (73%)
  starting transfers between devices  28.8 us (8%)
  other arithmetic  21.1 us (6%)
  between operations  15 us (4%)
  blocking collectives  13.3 us (4%)
  matrix products  10.8 us (3%)
  local copies, waits for them, and re-layouts  10.4 us (3%)
    psum x1, waiting for transfers between devices, body(): totals = lax.psum(padded, everyone)[:partials.shape[0]] / replicas  126 us
    unnamed x3, waiting for transfers between devices  89.2 us
    ppermute x4, waiting for transfers between devices, island_sum(): arrived = lax.ppermute(part, 'island', [(0, 1), (3, 2)])  27.2 us
    ppermute x4, waiting for transfers between devices, island_sum(): back = lax.ppermute(whole, 'island', [(1, 0), (2, 3)])  19.6 us
    ppermute x4, starting transfers between devices, island_sum(): arrived = lax.ppermute(part, 'island', [(0, 1), (3, 2)])  17.6 us
    psum x1, blocking collectives, body(): squares = lax.psum(jnp.sum(gradient * gradient), ('chip', 'core'))  13.3 us
    dot_general x1, matrix products, body(): lax.dot_general(their_unrotated, their_tokens, contract, preferred_elemen...  7.87 us
  transfers between devices with their start and end apart: 16, of which 9 were waited for; matrix products, arithmetic and copies ran while one was open for 4% of the time, Pallas kernels for 0%

commit v1 on v0

--- a/solution.py
+++ b/solution.py
@@ -17,6 +17,11 @@
 adam_eps = 1e-08
 norm_epsilon = 1e-06
 rope_base = 500000.0
+
+
+def add_all(x, mesh_axis):
+    terms = lax.all_gather(x, mesh_axis)
+    return jnp.sum(terms, axis=0)
 
 
 def unrotate(cotangent, first_row):
@@ -118,7 +123,7 @@
     everyone = ("island", "chip", "core")
     partials = local_tiles(island_drift, tile_rows, first_row)
     padded = jnp.zeros((65536,), jnp.float32).at[: partials.shape[0]].set(partials)
-    totals = lax.psum(padded, everyone)[: partials.shape[0]] / replicas
+    totals = add_all(padded, everyone)[: partials.shape[0]] / replicas
     drift = island_sum(island_drift, replicas) / replicas
     momentum_out = outer_moment * momentum + drift
     master_out = master - outer_rate * (drift + outer_moment * momentum_out)

time: 365 us -> 293 us (0.80)
  waiting for transfers between devices: 265 us -> 190 us
  other arithmetic: 21.1 us -> 25.4 us
    psum x1 -> x0, waiting for transfers between devices: 126 us -> none  [body(): totals = lax.psum(padded, everyone)[:partials.shape[0]] / replicas]
    ppermute x4, waiting for transfers between devices: 27.2 us -> 67.4 us  [island_sum(): arrived = lax.ppermute(part, 'island', [(0, 1), (3, 2)])]
    ppermute x4, waiting for transfers between devices: 19.6 us -> 32 us  [island_sum(): back = lax.ppermute(whole, 'island', [(1, 0), (2, 3)])]
    reduce_sum x0 -> x1, other arithmetic: none -> 6.34 us  [add_all(): return jnp.sum(terms, axis=0)]
  transfers between devices with their start and end apart: 16 -> 16, of which waited for: 9 -> 9; matrix products, arithmetic and copies ran while one was open for 4% -> 5% of each run, Pallas kernels for 0% -> 0%
where the time goes in v1:
time: 293 us; the launch traced here: 292 us
  waiting for transfers between devices  190 us (65%)
  starting transfers between devices  25.5 us (9%)
  other arithmetic  25.4 us (9%)
  between operations  15.1 us (5%)
  blocking collectives  13.3 us (5%)
  local copies, waits for them, and re-layouts  12.2 us (4%)
  matrix products  10.8 us (4%)
    unnamed x3, waiting for transfers between devices  88.3 us
    ppermute x4, waiting for transfers between devices, island_sum(): arrived = lax.ppermute(part, 'island', [(0, 1), (3, 2)])  67.4 us
    ppermute x4, waiting for transfers between devices, island_sum(): back = lax.ppermute(whole, 'island', [(1, 0), (2, 3)])  32 us
    ppermute x4, starting transfers between devices, island_sum(): arrived = lax.ppermute(part, 'island', [(0, 1), (3, 2)])  16.7 us
    psum x1, blocking collectives, body(): squares = lax.psum(jnp.sum(gradient * gradient), ('chip', 'core'))  13.3 us
    dot_general x1, matrix products, body(): lax.dot_general(their_unrotated, their_tokens, contract, preferred_elemen...  7.87 us
    reduce_sum x1, other arithmetic, local_tiles(): jnp.sum(drift_rows, axis=1)  6.65 us
    reduce_sum x1, other arithmetic, add_all(): return jnp.sum(terms, axis=0)  6.34 us
  transfers between devices with their start and end apart: 16, of which 9 were waited for; matrix products, arithmetic and copies ran while one was open for 5% of the time, Pallas kernels for 0%

profile of v1, /device:TPU:0, one launch (start us, length us, event | category | flops | bytes accessed | tf_op | source)
XLA Modules:
  0.0 292.1 jit_solution(3682787724836974566)
XLA Ops:
  7.2 5.7 %dynamic-slice_bitcast_fusion.3 = (bf16[512,1,1024]{2,0,1:T(8,128)(2,1)S(1)}, bf16[512,1,1024]{2,0,1:T(8,128)(2,1)S(1)}, bf16[512,1,1024]{2,0,1:T(8,128)(2,1)S(1...) fusion(bf16[1,512,8192]{2,1,0:T(8,128)(2,1)} %param.10, ...), kind=kLoop, calls=%fused_computation.31 | loop fusion | bytes 16777248 | tf_op jit(solution)/shard_map/stack | solution.py:98
  13.0 2.2 pad_maximum_fusion
  15.2 0.5 collective-permute-start.1
  15.6 1.3 copy.29
  16.9 0.5 multiply_cosine_fusion
  17.5 0.2 add_convert_fusion
  17.7 0.1 collective-permute-start
  17.8 0.3 copy-done.2
  18.1 0.3 copy-done.3
  18.4 2.5 fusion
  20.9 2.2 collective-permute-done
  23.1 7.9 %convolution_add_fusion = f32[512,4,1024]{2,0,1:T(8,128)} fusion(f32[512,4,1024]{2,0,1:T(8,128)S(1)} %fusion, bf16[512,4,1024]{2,0,1:T(8,128)(2,1)} %collective-permute-done.1, bf16[512,512]{0,1:T(8,128)(2,1)S(1)} %collective-permute-done), kind=kOutput, calls=%fused_computation.10 | convolution fusion | flops 2149580800 | bytes 21495808 | tf_op jit(solution)/shard_map/dot_general | solution.py:111
  31.1 0.6 copy-done.4
  31.7 0.1 copy.27
  31.8 0.1 reduce.3
  32.0 88.3 %reduce-scatter.4.cloned.1.call-done = f32[512,1,1024]{2,0,1:T(8,128)} async-done(((f32[512,4,1024]{2,0,1:T(8,128)}), f32[512,1,1024]{2,0,1:T(8,128)}) %reduce-scatter.4.cloned.1.call-update) | async-done | bytes 2097168
  120.2 1.9 copy.26
  122.1 1.1 fusion.14
  123.3 13.3 %psum.7 = f32[]{:T(128)} all-reduce(f32[]{:T(128)} %fusion.14), channel_id=1, replica_groups=mesh['island'=4,'chip'=4,'core'=2] {'chip','core'}, use_global_device_ids=true, to_apply=%region_2.3 | all-reduce | flops 1 | bytes 8 | tf_op jit(solution)/shard_map/psum | solution.py:117
  137.3 6.6 %fusion.26 = (f32[1024]{0:T(1024)S(1)}, f32[1024,512]{1,0:T(8,128)}) fusion(f32[1024,512]{1,0:T(8,128)} %param.12, f32[1,1024,512]{2,1,0:T(8,128)} %param.16, f32[]{:T(128)S(6)} %sqrt.9, f32[512,1,1024]{0,2,1:T(8,128)S(1)} %copy.26, f32[1,1024,512]{2,1,0:T(8,128)} %param.15, f32[1,1024,512]{2,1,0:T(8,128)} %param.14), kind=kLoop, calls=%fused_computation.63 | loop fusion | flops 9436160 | bytes 12587012 | tf_op jit(solution)/shard_map/reduce_sum | solution.py:56
  143.9 0.4 fusion.18
  144.3 0.9 pad_bitcast_fusion
  145.2 1.1 slice.41
  146.2 3.4 %collective-permute-start.2 = (f32[256,512]{1,0:T(8,128)S(1)}, f32[256,512]{1,0:T(8,128)S(1)}, u32[]{:S(2)}, u32[]{:S(2)}) collective-permute-start(f32[256,512]{1,0:T(8,128)S(1)} %slice.41), channel_id=1, source_target_pairs={{0,8},{24,16},{1,9},{25,17},{2,10},{26,18},{3,11},{27,19},{4,12},{... | collective-permute-start | bytes 1572872 | tf_op jit(solution)/shard_map/ppermute | solution.py:70
  149.7 15.2 %collective-permute-done.2 = f32[256,512]{1,0:T(8,128)S(1)} collective-permute-done((f32[256,512]{1,0:T(8,128)S(1)}, f32[256,512]{1,0:T(8,128)S(1)}, u32[]{:S(2)}, u32[]{:S(2)}) %collective-permute-start.2) | collective-permute-done | bytes 524320 | tf_op jit(solution)/shard_map/ppermute | solution.py:70
  164.9 1.8 slice_add_fusion
  166.7 4.4 %collective-permute-start.5 = (f32[256,512]{1,0:T(8,128)S(1)}, f32[256,512]{1,0:T(8,128)S(1)}, u32[]{:S(2)}, u32[]{:S(2)}) collective-permute-start(f32[256,512]{1,0:T(8,128)S(1)} %get-tuple-element.18), channel_id=1, source_target_pairs={{0,8},{24,16},{1,9},{25,17},{2,10},{26,18},{3,11},{27,19},{4,12},{... | collective-permute-start | bytes 1572872 | tf_op jit(solution)/shard_map/ppermute | solution.py:70
  171.1 21.1 %collective-permute-done.5 = f32[256,512]{1,0:T(8,128)S(1)} collective-permute-done((f32[256,512]{1,0:T(8,128)S(1)}, f32[256,512]{1,0:T(8,128)S(1)}, u32[]{:S(2)}, u32[]{:S(2)}) %collective-permute-start.5) | collective-permute-done | bytes 524320 | tf_op jit(solution)/shard_map/ppermute | solution.py:70
  192.3 4.4 %collective-permute-start.8 = (f32[256,512]{1,0:T(8,128)S(1)}, f32[256,512]{1,0:T(8,128)S(1)}, u32[]{:S(2)}, u32[]{:S(2)}) collective-permute-start(f32[256,512]{1,0:T(8,128)S(1)} %get-tuple-element.19), channel_id=1, source_target_pairs={{0,8},{24,16},{1,9},{25,17},{2,10},{26,18},{3,11},{27,19},{4,12},{... | collective-permute-start | bytes 1572872 | tf_op jit(solution)/shard_map/ppermute | solution.py:70
  196.7 0.7 collective-permute-start.3
  197.4 15.8 %collective-permute-done.8 = f32[256,512]{1,0:T(8,128)S(1)} collective-permute-done((f32[256,512]{1,0:T(8,128)S(1)}, f32[256,512]{1,0:T(8,128)S(1)}, u32[]{:S(2)}, u32[]{:S(2)}) %collective-permute-start.8) | collective-permute-done | bytes 524320 | tf_op jit(solution)/shard_map/ppermute | solution.py:70
  213.2 4.4 %collective-permute-start.11 = (f32[256,512]{1,0:T(8,128)S(1)}, f32[256,512]{1,0:T(8,128)S(1)}, u32[]{:S(2)}, u32[]{:S(2)}) collective-permute-start(f32[256,512]{1,0:T(8,128)S(1)} %get-tuple-element.20), channel_id=1, source_target_pairs={{0,8},{24,16},{1,9},{25,17},{2,10},{26,18},{3,11},{27,19},{4,12},{... | collective-permute-start | bytes 1572872 | tf_op jit(solution)/shard_map/ppermute | solution.py:70
  217.7 0.7 collective-permute-start.6
  218.5 0.7 collective-permute-start.9
  219.3 1.3 collective-permute-start.4
  220.6 15.3 %collective-permute-done.11 = f32[256,512]{1,0:T(8,128)S(1)} collective-permute-done((f32[256,512]{1,0:T(8,128)S(1)}, f32[256,512]{1,0:T(8,128)S(1)}, u32[]{:S(2)}, u32[]{:S(2)}) %collective-permute-start.11) | collective-permute-done | bytes 524320 | tf_op jit(solution)/shard_map/ppermute | solution.py:70
  235.9 0.7 collective-permute-start.12
  236.7 1.3 collective-permute-start.7
  238.2 1.3 collective-permute-start.10
  239.5 1.1 broadcast_select_fusion.3
  240.7 1.6 collective-permute-start.13
  242.3 12.6 %collective-permute-done.7 = f32[256,512]{1,0:T(8,128)} collective-permute-done((f32[256,512]{1,0:T(8,128)S(1)}, f32[256,512]{1,0:T(8,128)}, u32[]{:S(2)}, u32[]{:S(2)}) %collective-permute-start.7) | collective-permute-done | bytes 524320 | tf_op jit(solution)/shard_map/ppermute | solution.py:73
  254.9 1.1 broadcast_select_fusion.2
  256.0 9.7 %collective-permute-done.10 = f32[256,512]{1,0:T(8,128)S(1)} collective-permute-done((f32[256,512]{1,0:T(8,128)S(1)}, f32[256,512]{1,0:T(8,128)S(1)}, u32[]{:S(2)}, u32[]{:S(2)}) %collective-permute-start.10) | collective-permute-done | bytes 524320 | tf_op jit(solution)/shard_map/ppermute | solution.py:73
  265.9 9.6 %collective-permute-done.13 = f32[256,512]{1,0:T(8,128)S(1)} collective-permute-done((f32[256,512]{1,0:T(8,128)S(1)}, f32[256,512]{1,0:T(8,128)S(1)}, u32[]{:S(2)}, u32[]{:S(2)}) %collective-permute-start.13) | collective-permute-done | bytes 524320 | tf_op jit(solution)/shard_map/ppermute | solution.py:73
  275.6 2.8 multiply_subtract_fusion
  278.4 6.3 %reduce_sum.29 = f32[65536]{0:T(1024)S(1)} reduce(f32[32,1,65536]{2,1,0:T(1,128)} %all-gather.3.cloned.1.call-done, f32[]{:T(128)} %constant.108.clone.1), dimensions={0,1}, to_apply=%region_5.6 | reduce | flops 2031616 | bytes 8650756 | tf_op jit(solution)/shard_map/reduce_sum | solution.py:24
  284.7 0.5 fusion.24
  (33 shorter events, 1.0 us)
Async XLA Ops:
  7.2 113.1 %reduce-scatter.4.cloned.1.call-start = ((), (), s32[]{:S(2)}) async-start(), calls=%async_computation.2 | async-start | bytes 10485760
  15.2 8.0 %collective-permute-start.1 = (bf16[512,4,1024]{2,0,1:T(8,128)(2,1)}, bf16[512,4,1024]{2,0,1:T(8,128)(2,1)}, u32[]{:S(2)}, u32[]{:S(2)}) collective-permute-start(bf16[512,4,1024]{2,0,1:T(8,128)(2,1)} %pad_maximum_fusion), channel_id=1, source_target_pairs={{0,1},{1,0},{2,3},{3,2},{4,5},{5,4},{6,7},{7,6},{8,9},{9,8},{10,11... | collective-permute-start | bytes 12582920 | tf_op jit(solution)/shard_map/ppermute | solution.py:106
  16.9 1.2 copy-start.2
  16.9 1.5 copy-start.3
  17.7 5.5 %collective-permute-start = (bf16[512,512]{0,1:T(8,128)(2,1)S(1)}, bf16[512,512]{0,1:T(8,128)(2,1)S(1)}, u32[]{:S(2)}, u32[]{:S(2)}) collective-permute-start(bf16[512,512]{0,1:T(8,128)(2,1)S(1)} %bitcast.67), channel_id=1, source_target_pairs={{0,1},{1,0},{2,3},{3,2},{4,5},{5,4},{6,7},{7,6},{8,9},{9,8},{10,11... | collective-permute-start | bytes 1572872 | tf_op jit(solution)/shard_map/ppermute | solution.py:107
  31.0 0.7 copy-start.4
  31.0 247.3 %all-gather.3.cloned.1.call-start = ((), (), s32[]{:S(2)}) async-start(), calls=%async_computation.1 | async-start | bytes 8650752 | tf_op jit(solution)/shard_map/all_gather | solution.py:23
  146.2 18.6 %collective-permute-start.2 = (f32[256,512]{1,0:T(8,128)S(1)}, f32[256,512]{1,0:T(8,128)S(1)}, u32[]{:S(2)}, u32[]{:S(2)}) collective-permute-start(f32[256,512]{1,0:T(8,128)S(1)} %slice.41), channel_id=1, source_target_pairs={{0,8},{24,16},{1,9},{25,17},{2,10},{26,18},{3,11},{27,19},{4,12},{... | collective-permute-start | bytes 1572872 | tf_op jit(solution)/shard_map/ppermute | solution.py:70
  166.7 25.6 %collective-permute-start.5 = (f32[256,512]{1,0:T(8,128)S(1)}, f32[256,512]{1,0:T(8,128)S(1)}, u32[]{:S(2)}, u32[]{:S(2)}) collective-permute-start(f32[256,512]{1,0:T(8,128)S(1)} %get-tuple-element.18), channel_id=1, source_target_pairs={{0,8},{24,16},{1,9},{25,17},{2,10},{26,18},{3,11},{27,19},{4,12},{... | collective-permute-start | bytes 1572872 | tf_op jit(solution)/shard_map/ppermute | solution.py:70
  192.3 20.9 %collective-permute-start.8 = (f32[256,512]{1,0:T(8,128)S(1)}, f32[256,512]{1,0:T(8,128)S(1)}, u32[]{:S(2)}, u32[]{:S(2)}) collective-permute-start(f32[256,512]{1,0:T(8,128)S(1)} %get-tuple-element.19), channel_id=1, source_target_pairs={{0,8},{24,16},{1,9},{25,17},{2,10},{26,18},{3,11},{27,19},{4,12},{... | collective-permute-start | bytes 1572872 | tf_op jit(solution)/shard_map/ppermute | solution.py:70
  196.7 22.5 %collective-permute-start.3 = (f32[256,512]{1,0:T(8,128)S(1)}, f32[256,512]{1,0:T(8,128)S(1)}, u32[]{:S(2)}, u32[]{:S(2)}) collective-permute-start(f32[256,512]{1,0:T(8,128)S(1)} %get-tuple-element.33), channel_id=1, source_target_pairs={{8,16},{16,8},{9,17},{17,9},{10,18},{18,10},{11,19},{19,11},{12,20... | collective-permute-start | bytes 1572872 | tf_op jit(solution)/shard_map/ppermute | solution.py:72
  213.2 22.7 %collective-permute-start.11 = (f32[256,512]{1,0:T(8,128)S(1)}, f32[256,512]{1,0:T(8,128)S(1)}, u32[]{:S(2)}, u32[]{:S(2)}) collective-permute-start(f32[256,512]{1,0:T(8,128)S(1)} %get-tuple-element.20), channel_id=1, source_target_pairs={{0,8},{24,16},{1,9},{25,17},{2,10},{26,18},{3,11},{27,19},{4,12},{... | collective-permute-start | bytes 1572872 | tf_op jit(solution)/shard_map/ppermute | solution.py:70
  217.7 19.0 %collective-permute-start.6 = (f32[256,512]{1,0:T(8,128)S(1)}, f32[256,512]{1,0:T(8,128)S(1)}, u32[]{:S(2)}, u32[]{:S(2)}) collective-permute-start(f32[256,512]{1,0:T(8,128)S(1)} %add.168), channel_id=1, source_target_pairs={{8,16},{16,8},{9,17},{17,9},{10,18},{18,10},{11,19},{19,11},{12,20... | collective-permute-start | bytes 1572872 | tf_op jit(solution)/shard_map/ppermute | solution.py:72
  218.5 19.6 %collective-permute-start.9 = (f32[256,512]{1,0:T(8,128)S(1)}, f32[256,512]{1,0:T(8,128)S(1)}, u32[]{:S(2)}, u32[]{:S(2)}) collective-permute-start(f32[256,512]{1,0:T(8,128)S(1)} %add.170), channel_id=1, source_target_pairs={{8,16},{16,8},{9,17},{17,9},{10,18},{18,10},{11,19},{19,11},{12,20... | collective-permute-start | bytes 1572872 | tf_op jit(solution)/shard_map/ppermute | solution.py:72
  219.3 20.2 %collective-permute-start.4 = (f32[256,512]{1,0:T(8,128)S(1)}, f32[256,512]{1,0:T(8,128)}, u32[]{:S(2)}, u32[]{:S(2)}) collective-permute-start(f32[256,512]{1,0:T(8,128)S(1)} %add.167), channel_id=1, source_target_pairs={{8,0},{16,24},{9,1},{17,25},{10,2},{18,26},{11,3},{19,27},{12,4},{... | collective-permute-start | bytes 1572872 | tf_op jit(solution)/shard_map/ppermute | solution.py:73
  235.9 4.7 %collective-permute-start.12 = (f32[256,512]{1,0:T(8,128)S(1)}, f32[256,512]{1,0:T(8,128)S(1)}, u32[]{:S(2)}, u32[]{:S(2)}) collective-permute-start(f32[256,512]{1,0:T(8,128)S(1)} %add.172), channel_id=1, source_target_pairs={{8,16},{16,8},{9,17},{17,9},{10,18},{18,10},{11,19},{19,11},{12,20... | collective-permute-start | bytes 1572872 | tf_op jit(solution)/shard_map/ppermute | solution.py:72
  236.7 18.2 %collective-permute-start.7 = (f32[256,512]{1,0:T(8,128)S(1)}, f32[256,512]{1,0:T(8,128)}, u32[]{:S(2)}, u32[]{:S(2)}) collective-permute-start(f32[256,512]{1,0:T(8,128)S(1)} %add.169), channel_id=1, source_target_pairs={{8,0},{16,24},{9,1},{17,25},{10,2},{18,26},{11,3},{19,27},{12,4},{... | collective-permute-start | bytes 1572872 | tf_op jit(solution)/shard_map/ppermute | solution.py:73
  238.2 27.6 %collective-permute-start.10 = (f32[256,512]{1,0:T(8,128)S(1)}, f32[256,512]{1,0:T(8,128)S(1)}, u32[]{:S(2)}, u32[]{:S(2)}) collective-permute-start(f32[256,512]{1,0:T(8,128)S(1)} %add.171), channel_id=1, source_target_pairs={{8,0},{16,24},{9,1},{17,25},{10,2},{18,26},{11,3},{19,27},{12,4},{... | collective-permute-start | bytes 1572872 | tf_op jit(solution)/shard_map/ppermute | solution.py:73
  240.7 34.8 %copy-start = (f32[1024,512]{1,0:T(8,128)S(1)}, f32[1024,512]{1,0:T(8,128)}, u32[]{:S(2)}) copy-start(f32[1024,512]{1,0:T(8,128)} %param.12) | copy-start | bytes 6291460
  240.7 34.8 %copy-start.1 = (f32[1024,512]{1,0:T(8,128)S(1)}, f32[1024,512]{1,0:T(8,128)}, u32[]{:S(2)}) copy-start(f32[1024,512]{1,0:T(8,128)} %param.13) | copy-start | bytes 6291460
  240.7 34.7 %collective-permute-start.13 = (f32[256,512]{1,0:T(8,128)S(1)}, f32[256,512]{1,0:T(8,128)S(1)}, u32[]{:S(2)}, u32[]{:S(2)}) collective-permute-start(f32[256,512]{1,0:T(8,128)S(1)} %add.173), channel_id=1, source_target_pairs={{8,0},{16,24},{9,1},{17,25},{10,2},{18,26},{11,3},{19,27},{12,4},{... | collective-permute-start | bytes 1572872 | tf_op jit(solution)/shard_map/ppermute | solution.py:73
Sparse Core Ops, SparseCore 0:
  31.2 89.0 reduce-scatter.3
  145.3 93.9 all-gather.2
